TPU v7x, 256 devices: a whole 4x4x8 slice. The times are simulated.
256 devices in a mesh: req: 32 (over z, x_hi, core), mlp: 8 (over x_lo, y).
Axes of the slice: x: 4 (x_hi: 2, x_lo: 2; x = x_hi * 2 + x_lo), y: 4, z: 8, core: 2. Of those that a mesh axis runs over, the one named last changes fastest.
Arguments:
- residual_in: bfloat16 [1024, 2560], P('req'), may hold values from -6 to 6
- queries: bfloat16 [1024, 2560], P('req', 'mlp')
- fresh_rotated_keys: bfloat16 [1024, 640], P('req', 'mlp'), may hold values from -6 to 6
- fresh_value_rows: bfloat16 [1024, 640], P('req', 'mlp'), may hold values from -6 to 6
- shared_prefix_keys: bfloat16 [32, 16384, 640], P(None, 'req', 'mlp'), may hold values from -6 to 6
- shared_prefix_values: bfloat16 [32, 16384, 640], P(None, 'req', 'mlp'), may hold values from -6 to 6
- sample_tail_keys: bfloat16 [32, 16, 128, 640], P('req', None, None, 'mlp'), may hold values from -6 to 6
- sample_tail_values: bfloat16 [32, 16, 128, 640], P('req', None, None, 'mlp'), may hold values from -6 to 6
- prompt_prefix_length: int32 [32], replicated, may hold values from 1 to 16384, as said below
- sample_tail_length: int32 [32, 16], P('req'), may hold values from 0 to 128, as said below
- out_weight: bfloat16 [2560, 2560], P('mlp'), may hold values from -0.125 to 0.125
- gate_weight: bfloat16 [2560, 4096], P(None, 'mlp'), may hold values from -0.125 to 0.125
- up_weight: bfloat16 [2560, 4096], P(None, 'mlp'), may hold values from -0.125 to 0.125
- down_weight: bfloat16 [4096, 2560], P('mlp'), may hold values from -0.09375 to 0.09375
- mlp_gain: float32 [2560], replicated, may hold values from 0.1 to 1.9
- final_gain: float32 [2560], replicated, may hold values from 0.1 to 1.9
- score_weight: float32 [2560], replicated, may hold values from -0.125 to 0.125
Outputs:
- layer_out: bfloat16 [1024, 2560], P('req', 'mlp')
- score: float32 [1024], P('req')
Inputs may be any that keep to these rules, and one draw needn't show every extreme that they name: `prompt_prefix_length`: one prompt in every draw has the full prefix length 16384. `sample_tail_length`: one sample in every draw has the full tail length 128.
All inputs are finite; a program needn't handle non-finite values.
Results may differ from a plain program's by a relative error of at most 0.02.
Values may be sent and summed in bfloat16 or wider, within the bound.
No kernel may reach another device: no remote copies, remote signals or barrier semaphores. Data moves between devices by JAX's collectives and lax.ppermute only.
A program may use at most 128 MiB of HBM per device.

v0:
```python
import jax
import jax.numpy as jnp
from jax import lax
from jax.sharding import PartitionSpec as P

D = 2560
QUERY_HEADS = 32
KEY_VALUE_HEADS = 8
HEAD_SIZE = 80
SAMPLE_COUNT = 16
DECODE_TOKENS = 2
TAIL_LENGTH = 128


def rms_scale(total_sq, width):
    return lax.rsqrt(total_sq / width + 1e-05)


def on_device(
    residual_in,
    queries,
    fresh_rotated_keys,
    fresh_value_rows,
    shared_prefix_keys,
    shared_prefix_values,
    sample_tail_keys,
    sample_tail_values,
    prompt_prefix_length,
    sample_tail_length,
    out_weight,
    gate_weight,
    up_weight,
    down_weight,
    mlp_gain,
    final_gain,
    score_weight,
):
    query_groups = QUERY_HEADS // KEY_VALUE_HEADS
    inv_root = HEAD_SIZE ** (-0.5)
    kv_local = fresh_rotated_keys.shape[1] // HEAD_SIZE
    prompts = shared_prefix_keys.shape[0]
    piece_len = shared_prefix_keys.shape[1]
    req_index = lax.axis_index("req")
    low = jnp.float32(-1e30)
    gathered = lax.all_gather(queries, "req", axis=0, tiled=True)
    query_all = gathered.reshape(
        prompts, SAMPLE_COUNT, DECODE_TOKENS, kv_local, query_groups, HEAD_SIZE
    )
    prefix_key_block = shared_prefix_keys.reshape(prompts, piece_len, kv_local, HEAD_SIZE)
    prefix_value_block = shared_prefix_values.reshape(prompts, piece_len, kv_local, HEAD_SIZE)
    score_pre = (
        jnp.einsum(
            "psjkgh,plkh->pksjgl", query_all, prefix_key_block, preferred_element_type=jnp.float32
        )
        * inv_root
    )
    key_place = req_index * piece_len + jnp.arange(piece_len)
    valid = (key_place[None, :] < prompt_prefix_length[:, None])[:, None, None, None, None, :]
    piece_top = jnp.max(jnp.where(valid, score_pre, low), -1)
    piece_w = jnp.where(valid, jnp.exp(score_pre - piece_top[..., None]), 0.0)
    piece_sum = jnp.sum(piece_w, -1)
    piece_out = jnp.einsum(
        "pksjgl,plkh->pksjgh",
        piece_w.astype(jnp.bfloat16),
        prefix_value_block,
        preferred_element_type=jnp.float32,
    )
    source_out, source_top, source_sum = (
        lax.all_to_all(piece_out, "req", split_axis=0, concat_axis=0, tiled=True),
        lax.all_to_all(piece_top, "req", split_axis=0, concat_axis=0, tiled=True),
        lax.all_to_all(piece_sum, "req", split_axis=0, concat_axis=0, tiled=True),
    )
    query_own = queries.reshape(SAMPLE_COUNT, DECODE_TOKENS, kv_local, query_groups, HEAD_SIZE)
    tail_key_block = sample_tail_keys.reshape(SAMPLE_COUNT, TAIL_LENGTH, kv_local, HEAD_SIZE)
    tail_value_block = sample_tail_values.reshape(SAMPLE_COUNT, TAIL_LENGTH, kv_local, HEAD_SIZE)
    fresh_k = fresh_rotated_keys.reshape(SAMPLE_COUNT, DECODE_TOKENS, kv_local, HEAD_SIZE)
    fresh_v = fresh_value_rows.reshape(SAMPLE_COUNT, DECODE_TOKENS, kv_local, HEAD_SIZE)
    score_tail = (
        jnp.einsum(
            "sjkgh,stkh->ksjgt", query_own, tail_key_block, preferred_element_type=jnp.float32
        )
        * inv_root
    )
    score_new = (
        jnp.einsum("sjkgh,sikh->ksjgi", query_own, fresh_k, preferred_element_type=jnp.float32)
        * inv_root
    )
    mask_tail = (jnp.arange(TAIL_LENGTH)[None, :] < sample_tail_length[0][:, None])[
        None, :, None, None, :
    ]
    causal = (jnp.arange(DECODE_TOKENS)[None, :] <= jnp.arange(DECODE_TOKENS)[:, None])[
        None, None, :, None, :
    ]
    local_top = jnp.maximum(
        jnp.max(jnp.where(mask_tail, score_tail, low), -1),
        jnp.max(jnp.where(causal, score_new, low), -1),
    )
    w_tail = jnp.where(mask_tail, jnp.exp(score_tail - local_top[..., None]), 0.0)
    w_new = jnp.where(causal, jnp.exp(score_new - local_top[..., None]), 0.0)
    local_sum = jnp.sum(w_tail, -1) + jnp.sum(w_new, -1)
    local_out = jnp.einsum(
        "ksjgt,stkh->ksjgh",
        w_tail.astype(jnp.bfloat16),
        tail_value_block,
        preferred_element_type=jnp.float32,
    )
    local_out = local_out + jnp.einsum(
        "ksjgi,sikh->ksjgh", w_new.astype(jnp.bfloat16), fresh_v, preferred_element_type=jnp.float32
    )
    overall = jnp.maximum(jnp.max(source_top, 0), local_top)
    source_w = jnp.exp(source_top - overall[None])
    local_w = jnp.exp(local_top - overall)
    numer = jnp.sum(source_w[..., None] * source_out, 0) + local_w[..., None] * local_out
    denom = jnp.sum(source_w * source_sum, 0) + local_w * local_sum
    attention_layer = (numer / denom[..., None]).astype(jnp.bfloat16)
    attention_layer = jnp.transpose(attention_layer, (1, 2, 0, 3, 4)).reshape(
        SAMPLE_COUNT * DECODE_TOKENS, kv_local * query_groups * HEAD_SIZE
    )
    projected = jnp.dot(attention_layer, out_weight, preferred_element_type=jnp.float32)
    mlp_count = lax.axis_size("mlp")
    mlp_index = lax.axis_index("mlp")
    share = D // mlp_count
    mid = residual_in.astype(jnp.float32) + lax.psum(projected.astype(jnp.bfloat16), "mlp").astype(
        jnp.float32
    )
    normed = (mid * rms_scale(jnp.sum(mid * mid, -1, keepdims=True), D) * mlp_gain).astype(
        jnp.bfloat16
    )
    gate = jnp.dot(normed, gate_weight, preferred_element_type=jnp.float32)
    upper = jnp.dot(normed, up_weight, preferred_element_type=jnp.float32)
    hidden = (jax.nn.silu(gate) * upper).astype(jnp.bfloat16)
    stream = mid + lax.psum(
        jnp.dot(hidden, down_weight, preferred_element_type=jnp.float32).astype(jnp.bfloat16), "mlp"
    ).astype(jnp.float32)
    score = jnp.sum(
        stream
        * rms_scale(jnp.sum(stream * stream, -1, keepdims=True), D)
        * final_gain
        * score_weight,
        -1,
    )
    layer_out = lax.dynamic_slice_in_dim(stream, mlp_index * share, share, 1).astype(jnp.bfloat16)
    return (layer_out, score)


def solution(mesh):
    placed = (
        P("req", None),
        P("req", "mlp"),
        P("req", "mlp"),
        P("req", "mlp"),
        P(None, "req", "mlp"),
        P(None, "req", "mlp"),
        P("req", None, None, "mlp"),
        P("req", None, None, "mlp"),
        P(),
        P("req", None),
        P("mlp", None),
        P(None, "mlp"),
        P(None, "mlp"),
        P("mlp", None),
        P(),
        P(),
        P(),
    )
    return jax.shard_map(
        on_device,
        mesh=mesh,
        in_specs=placed,
        out_specs=(P("req", "mlp"), P("req")),
        check_vma=False,
    )
```

profile of v0, /device:TPU:6, one launch (start us, length us, event | category | flops | bytes accessed | tf_op | source)
XLA Modules:
  0.0 322.3 jit_solution(5369909995095081894)
XLA Ops:
  7.2 43.4 %all_gather.3 = bf16[1024,320]{1,0:T(8,128)(2,1)S(1)} all-gather(bf16[32,320]{1,0:T(8,128)(2,1)} %param.18), channel_id=1, replica_groups=mesh['req'=32,'mlp'=8] {'req'}, dimensions={0}, use_global_device_ids=true | all-gather | bytes 675840 | tf_op jit(solution)/shard_map/all_gather | solution.py:45
  50.6 1.6 reshape.254
  52.4 2.8 select_reduce_fusion
  55.2 2.3 fusion
  57.4 0.9 copy-done.1
  58.4 0.7 reshape.268
  59.1 8.4 %all-to-all-start.2 = ((f32[32,1,128]{2,1,0:T(1,128)}), f32[32,1,128]{2,1,0:T(1,128)S(1)}, u32[]{:S(2)}, u32[]{:S(2)}) async-start(f32[32,1,128]{2,1,0:T(1,128)} %reshape.268), calls=%async_computation.2 | async-start | bytes 32768 | tf_op jit(solution)/shard_map/all_to_all | solution.py:71
  67.6 0.7 reshape.266
  68.3 6.4 %all-to-all-done.2 = f32[32,1,128]{2,1,0:T(1,128)S(1)} async-done(((f32[32,1,128]{2,1,0:T(1,128)}), f32[32,1,128]{2,1,0:T(1,128)S(1)}, u32[]{:S(2)}, u32[]{:S(2)}) %all-to-all-start.2) | async-done | bytes 16416 | tf_op jit(solution)/shard_map/all_to_all | solution.py:71
  74.7 6.3 %all-to-all-start = ((f32[32,1,128]{2,1,0:T(1,128)}), f32[32,1,128]{2,1,0:T(1,128)S(1)}, u32[]{:S(2)}, u32[]{:S(2)}) async-start(f32[32,1,128]{2,1,0:T(1,128)} %reshape.266), calls=%async_computation | async-start | bytes 32768 | tf_op jit(solution)/shard_map/all_to_all | solution.py:70
  81.0 7.2 %fusion.11 = f32[32,1,16,2,4,80]{5,2,4,3,1,0:T(8,128)} fusion(bf16[32,512,80]{1,2,0:T(8,128)(2,1)} %param.22, f32[32,16,2,4,512]{4,1,3,2,0:T(8,128)} %copy-done.1, f32[32,16,2,4]{1,3,2,0:T(4,128)S(1)} %get-tuple-element.8, pred[32,512]{1,0:T(8,128)(4,1)S(1)} %broadcast_compare_fusion), kind=kOutput, calls=%fused_computation.15 | convolution fusion | flops 343932928 | bytes 12353536 | tf_op jit(solution)/shard_map/pksjgl,plkh->pksjgh/dot_general | solution.py:62
  88.3 10.1 %all-to-all-start.1 = ((f32[32,1,16,2,4,80]{5,2,4,3,1,0:T(8,128)}), f32[32,1,16,2,4,80]{5,2,4,3,1,0:T(8,128)}, u32[]{:S(2)}, u32[]{:S(2)}) async-start(f32[32,1,16,2,4,80]{5,2,4,3,1,0:T(8,128)} %fusion.11), calls=%async_computation.1 | async-start | bytes 4194304 | tf_op jit(solution)/shard_map/all_to_all | solution.py:69
  101.6 0.7 reduce.16
  103.1 45.6 %all-to-all-done.1 = f32[32,1,16,2,4,80]{5,2,4,3,1,0:T(8,128)} async-done(((f32[32,1,16,2,4,80]{5,2,4,3,1,0:T(8,128)}), f32[32,1,16,2,4,80]{5,2,4,3,1,0:T(8,128)}, u32[]{:S(2)}, u32[]{:S(2)}) %all-to-all-start.1) | async-done | bytes 1310752 | tf_op jit(solution)/shard_map/all_to_all | solution.py:69
  148.7 1.9 bitcast_reduce_fusion
  151.0 2.5 convolution_convert_fusion.1
  153.6 74.1 %all-reduce.3.cloned.1.call-done = bf16[32,2560]{1,0:T(8,128)(2,1)} async-done(((bf16[32,2560]{1,0:T(8,128)(2,1)}), bf16[32,2560]{1,0:T(8,128)(2,1)}) %all-reduce.3.cloned.1.call-update) | async-done | bytes 163856 | tf_op jit(solution)/shard_map/psum | solution.py:123
  227.7 1.1 multiply_reduce_fusion.2
  228.9 2.4 fusion.45
  231.3 4.3 %convolution_convert_fusion = bf16[32,2560]{1,0:T(8,128)(2,1)} fusion(bf16[512,2560]{1,0:T(8,128)(2,1)} %param.30, bf16[2560,512]{1,0:T(8,128)(2,1)} %param.29, f32[32,512]{1,0:T(8,128)S(1)} %fusion.45, bf16[32,2560]{1,0:T(8,128)(2,1)S(1)} %copy-done.3, bf16[32,2560]{1,0:T(8,128)(2,1)S(1)} %copy-done.2, f32[2560]{0:T(1024)S(1)} %copy-done.6, ...), kind=kOutput, calls=%fused_computation.9 | convolution fusion | flops 168443904 | bytes 5810304 | tf_op jit(solution)/shard_map/dot_general | solution.py:133
  235.7 77.2 %all-reduce.5.cloned.1.call-done = bf16[32,2560]{1,0:T(8,128)(2,1)} async-done(((bf16[32,2560]{1,0:T(8,128)(2,1)}), bf16[32,2560]{1,0:T(8,128)(2,1)}) %all-reduce.5.cloned.1.call-update) | async-done | bytes 163856 | tf_op jit(solution)/shard_map/psum | solution.py:132
  312.9 1.1 multiply_reduce_fusion.1
  314.0 0.7 dynamic-slice_convert_fusion
  314.7 0.7 multiply_reduce_fusion
  (64 shorter events, 4.6 us)
Async XLA Ops:
  7.2 45.2 %copy-start = (bf16[32,512,80]{1,2,0:T(8,128)(2,1)S(1)}, bf16[32,512,80]{1,2,0:T(8,128)(2,1)}, u32[]{:S(2)}) copy-start(bf16[32,512,80]{1,2,0:T(8,128)(2,1)} %param.21) | copy-start | bytes 7864324
  7.2 45.1 %copy-start.9 = (s32[32]{0:T(128)S(1)}, s32[32]{0:T(128)}, u32[]{:S(2)}) copy-start(s32[32]{0:T(128)} %param.25) | copy-start | bytes 388
  55.2 3.2 copy-start.1
  59.1 15.6 %all-to-all-start.2 = ((f32[32,1,128]{2,1,0:T(1,128)}), f32[32,1,128]{2,1,0:T(1,128)S(1)}, u32[]{:S(2)}, u32[]{:S(2)}) async-start(f32[32,1,128]{2,1,0:T(1,128)} %reshape.268), calls=%async_computation.2 | async-start | bytes 32768 | tf_op jit(solution)/shard_map/all_to_all | solution.py:71
  74.7 13.6 %all-to-all-start = ((f32[32,1,128]{2,1,0:T(1,128)}), f32[32,1,128]{2,1,0:T(1,128)S(1)}, u32[]{:S(2)}, u32[]{:S(2)}) async-start(f32[32,1,128]{2,1,0:T(1,128)} %reshape.266), calls=%async_computation | async-start | bytes 32768 | tf_op jit(solution)/shard_map/all_to_all | solution.py:70
  88.3 10.2 %copy-start.5 = (bf16[32,320]{1,0:T(8,128)(2,1)S(1)}, bf16[32,320]{1,0:T(8,128)(2,1)}, u32[]{:S(2)}) copy-start(bf16[32,320]{1,0:T(8,128)(2,1)} %param.18) | copy-start | bytes 61444
  88.3 10.3 %copy-start.12 = (bf16[32,80]{1,0:T(8,128)(2,1)S(1)}, bf16[32,80]{1,0:T(8,128)(2,1)}, u32[]{:S(2)}) copy-start(bf16[32,80]{1,0:T(8,128)(2,1)} %param.19) | copy-start | bytes 15364
  88.3 10.8 %copy-start.10 = (s32[1,16]{1,0:T(1,128)S(1)}, s32[1,16]{1,0:T(1,128)}, u32[]{:S(2)}) copy-start(s32[1,16]{1,0:T(1,128)} %param.26) | copy-start | bytes 196
  88.3 10.9 %copy-start.4 = (bf16[1,16,128,80]{2,3,1,0:T(8,128)(2,1)S(1)}, bf16[1,16,128,80]{2,3,1,0:T(8,128)(2,1)}, u32[]{:S(2)}) copy-start(bf16[1,16,128,80]{2,3,1,0:T(8,128)(2,1)} %param.23) | copy-start | bytes 983044
  88.3 14.5 %copy-start.11 = (bf16[1,16,128,80]{2,3,1,0:T(8,128)(2,1)S(1)}, bf16[1,16,128,80]{2,3,1,0:T(8,128)(2,1)}, u32[]{:S(2)}) copy-start(bf16[1,16,128,80]{2,3,1,0:T(8,128)(2,1)} %param.24) | copy-start | bytes 983044
  88.3 60.4 %all-to-all-start.1 = ((f32[32,1,16,2,4,80]{5,2,4,3,1,0:T(8,128)}), f32[32,1,16,2,4,80]{5,2,4,3,1,0:T(8,128)}, u32[]{:S(2)}, u32[]{:S(2)}) async-start(f32[32,1,16,2,4,80]{5,2,4,3,1,0:T(8,128)} %fusion.11), calls=%async_computation.1 | async-start | bytes 4194304 | tf_op jit(solution)/shard_map/all_to_all | solution.py:69
  98.4 129.3 %all-reduce.3.cloned.1.call-start = ((), (), s32[]{:S(2)}) async-start(), calls=%async_computation.3 | async-start | bytes 327680 | tf_op jit(solution)/shard_map/psum | solution.py:123
  99.0 51.7 %copy-start.13 = (bf16[32,80]{1,0:T(8,128)(2,1)S(1)}, bf16[32,80]{1,0:T(8,128)(2,1)}, u32[]{:S(2)}) copy-start(bf16[32,80]{1,0:T(8,128)(2,1)} %param.20) | copy-start | bytes 15364
  150.6 77.1 %copy-start.2 = (bf16[32,2560]{1,0:T(8,128)(2,1)S(1)}, bf16[32,2560]{1,0:T(8,128)(2,1)}, u32[]{:S(2)}) copy-start(bf16[32,2560]{1,0:T(8,128)(2,1)} %param.17) | copy-start | bytes 491524
  150.6 78.2 %copy-start.6 = (f32[2560]{0:T(1024)S(1)}, f32[2560]{0:T(1024)}, u32[]{:S(2)}) copy-start(f32[2560]{0:T(1024)} %param.31) | copy-start | bytes 30724
  153.5 159.4 %all-reduce.5.cloned.1.call-start = ((), (), s32[]{:S(2)}) async-start(), calls=%async_computation.4 | async-start | bytes 327680 | tf_op jit(solution)/shard_map/psum | solution.py:132
  227.7 3.6 %copy-start.3 = (bf16[32,2560]{1,0:T(8,128)(2,1)S(1)}, bf16[32,2560]{1,0:T(8,128)(2,1)}, u32[]{:S(2)}) copy-start(bf16[32,2560]{1,0:T(8,128)(2,1)} %all-reduce.3.cloned.1.call-done) | copy-start | bytes 491524
  231.3 83.4 %copy-start.7 = (f32[2560]{0:T(1024)S(1)}, f32[2560]{0:T(1024)}, u32[]{:S(2)}) copy-start(f32[2560]{0:T(1024)} %param.33) | copy-start | bytes 30724
  231.3 83.4 %copy-start.8 = (f32[2560]{0:T(1024)S(1)}, f32[2560]{0:T(1024)}, u32[]{:S(2)}) copy-start(f32[2560]{0:T(1024)} %param.32) | copy-start | bytes 30724
Sparse Core Ops, SparseCore 0:
  153.7 73.9 all-reduce.2
  235.8 77.0 all-reduce.4
where the time goes:
time: 323 us; the launch traced here: 322 us
  waiting for transfers between devices  203 us (63%)
  blocking collectives  43.4 us (13%)
  starting transfers between devices  24.9 us (8%)
  matrix products  20.6 us (6%)
  between operations  14.4 us (4%)
  other arithmetic  9.26 us (3%)
  local copies, waits for them, and re-layouts  6.46 us (2%)
    psum x1, waiting for transfers between devices, on_device(): lax.psum(jnp.dot(hidden, down_weight, preferred_element_type=jnp.float32)...  77.2 us
    psum x1, waiting for transfers between devices, on_device(): lax.psum(projected.astype(jnp.bfloat16), 'mlp').astype(jnp.float32)  74.1 us
    all_to_all x1, waiting for transfers between devices, on_device(): lax.all_to_all(piece_out, 'req', split_axis=0, concat_axis=0, tiled=True)  45.6 us
    all_gather x1, blocking collectives, on_device(): gathered = lax.all_gather(queries, 'req', axis=0, tiled=True)  43.4 us
    all_to_all x1, starting transfers between devices, on_device(): lax.all_to_all(piece_out, 'req', split_axis=0, concat_axis=0, tiled=True)  10.1 us
    all_to_all x1, starting transfers between devices, on_device(): lax.all_to_all(piece_sum, 'req', split_axis=0, concat_axis=0, tiled=True)  8.41 us
    dot_general x1, matrix products, on_device(): jnp.einsum('pksjgl,plkh->pksjgh', piece_w.astype(jnp.bfloat16), prefix_va...  7.23 us
  transfers between devices with their start and end apart: 5, of which 4 were waited for; matrix products, arithmetic and copies ran while one was open for 4% of the time, Pallas kernels for 0%

commit v1 on v0

--- a/solution.py
+++ b/solution.py
@@ -2,6 +2,7 @@
 import jax.numpy as jnp
 from jax import lax
 from jax.sharding import PartitionSpec as P
+from jax.lax import all_to_all, axis_size
 
 D = 2560
 QUERY_HEADS = 32
@@ -42,7 +43,10 @@
     piece_len = shared_prefix_keys.shape[1]
     req_index = lax.axis_index("req")
     low = jnp.float32(-1e30)
-    gathered = lax.all_gather(queries, "req", axis=0, tiled=True)
+    gathered = jnp.concatenate(
+        all_to_all(jnp.stack([queries for _ in range(axis_size("req"))], axis=0), "req", 0, 0),
+        axis=0,
+    )
     query_all = gathered.reshape(
         prompts, SAMPLE_COUNT, DECODE_TOKENS, kv_local, query_groups, HEAD_SIZE
     )

time: 323 us -> 313 us (0.969)
  blocking collectives: 43.4 us -> 0 us
  waiting for transfers between devices: 203 us -> 226 us
  starting transfers between devices: 24.9 us -> 33 us
    all_gather x1 -> x0, blocking collectives: 43.4 us -> none  [on_device(): gathered = lax.all_gather(queries, 'req', axis=0, tiled=True)]
    all_to_all x0 -> x1, waiting for transfers between devices: none -> 22.6 us  [on_device(): all_to_all(jnp.stack([queries for _ in range(axis_size('req'))], axis=0),...]
    all_to_all x0 -> x1, starting transfers between devices: none -> 11.6 us  [on_device(): all_to_all(jnp.stack([queries for _ in range(axis_size('req'))], axis=0),...]
    all_to_all x1, starting transfers between devices: 8.41 us -> 4.98 us  [on_device(): lax.all_to_all(piece_sum, 'req', split_axis=0, concat_axis=0, tiled=True)]
  transfers between devices with their start and end apart: 5 -> 6, of which waited for: 4 -> 5; matrix products, arithmetic and copies ran while one was open for 4% -> 4% of each run, Pallas kernels for 0% -> 0%
where the time goes in v1:
time: 313 us; the launch traced here: 312 us
  waiting for transfers between devices  226 us (72%)
  starting transfers between devices  33 us (11%)
  matrix products  20.6 us (7%)
  between operations  14.3 us (5%)
  other arithmetic  9.92 us (3%)
  local copies, waits for them, and re-layouts  8.28 us (3%)
    psum x1, waiting for transfers between devices, on_device(): lax.psum(jnp.dot(hidden, down_weight, preferred_element_type=jnp.float32)...  77.3 us
    psum x1, waiting for transfers between devices, on_device(): lax.psum(projected.astype(jnp.bfloat16), 'mlp').astype(jnp.float32)  74.4 us
    all_to_all x1, waiting for transfers between devices, on_device(): lax.all_to_all(piece_out, 'req', split_axis=0, concat_axis=0, tiled=True)  45.6 us
    all_to_all x1, waiting for transfers between devices, on_device(): all_to_all(jnp.stack([queries for _ in range(axis_size('req'))], axis=0),...  22.6 us
    all_to_all x1, starting transfers between devices, on_device(): all_to_all(jnp.stack([queries for _ in range(axis_size('req'))], axis=0),...  11.6 us
    all_to_all x1, starting transfers between devices, on_device(): lax.all_to_all(piece_out, 'req', split_axis=0, concat_axis=0, tiled=True)  10.1 us
    dot_general x1, matrix products, on_device(): jnp.einsum('pksjgl,plkh->pksjgh', piece_w.astype(jnp.bfloat16), prefix_va...  7.23 us
    all_to_all x1, waiting for transfers between devices, on_device(): lax.all_to_all(piece_sum, 'req', split_axis=0, concat_axis=0, tiled=True)  6.39 us
  transfers between devices with their start and end apart: 6, of which 5 were waited for; matrix products, arithmetic and copies ran while one was open for 4% of the time, Pallas kernels for 0%

profile of v1, /device:TPU:6, one launch (start us, length us, event | category | flops | bytes accessed | tf_op | source)
XLA Modules:
  0.0 312.4 jit_solution(2072827364197128077)
XLA Ops:
  7.2 1.8 stack.2
  9.0 11.6 %all-to-all-start = ((bf16[32,32,320]{2,1,0:T(8,128)(2,1)}), bf16[32,32,320]{2,1,0:T(8,128)(2,1)S(1)}, u32[]{:S(2)}, u32[]{:S(2)}) async-start(bf16[32,32,320]{2,1,0:T(8,128)(2,1)} %stack.2), calls=%async_computation | async-start | bytes 1572864 | tf_op jit(solution)/shard_map/all_to_all | solution.py:47
  21.4 22.6 %all-to-all-done = bf16[32,32,320]{2,1,0:T(8,128)(2,1)S(1)} async-done(((bf16[32,32,320]{2,1,0:T(8,128)(2,1)}), bf16[32,32,320]{2,1,0:T(8,128)(2,1)S(1)}, u32[]{:S(2)}, u32[]{:S(2)}) %all-to-all-start) | async-done | bytes 655392 | tf_op jit(solution)/shard_map/all_to_all | solution.py:47
  43.9 1.6 reshape.255
  45.6 2.8 select_reduce_fusion
  48.4 2.3 fusion
  50.6 0.9 copy-done.1
  51.6 0.7 reshape.269
  52.3 5.0 %all-to-all-start.3 = ((f32[32,1,128]{2,1,0:T(1,128)}), f32[32,1,128]{2,1,0:T(1,128)S(1)}, u32[]{:S(2)}, u32[]{:S(2)}) async-start(f32[32,1,128]{2,1,0:T(1,128)} %reshape.269), calls=%async_computation.3 | async-start | bytes 32768 | tf_op jit(solution)/shard_map/all_to_all | solution.py:75
  57.3 0.7 reshape.267
  58.1 6.4 %all-to-all-done.3 = f32[32,1,128]{2,1,0:T(1,128)S(1)} async-done(((f32[32,1,128]{2,1,0:T(1,128)}), f32[32,1,128]{2,1,0:T(1,128)S(1)}, u32[]{:S(2)}, u32[]{:S(2)}) %all-to-all-start.3) | async-done | bytes 16416 | tf_op jit(solution)/shard_map/all_to_all | solution.py:75
  64.5 6.3 %all-to-all-start.1 = ((f32[32,1,128]{2,1,0:T(1,128)}), f32[32,1,128]{2,1,0:T(1,128)S(1)}, u32[]{:S(2)}, u32[]{:S(2)}) async-start(f32[32,1,128]{2,1,0:T(1,128)} %reshape.267), calls=%async_computation.1 | async-start | bytes 32768 | tf_op jit(solution)/shard_map/all_to_all | solution.py:74
  70.8 7.2 %fusion.11 = f32[32,1,16,2,4,80]{5,2,4,3,1,0:T(8,128)} fusion(bf16[32,512,80]{1,2,0:T(8,128)(2,1)} %param.22, f32[32,16,2,4,512]{4,1,3,2,0:T(8,128)} %copy-done.1, f32[32,16,2,4]{1,3,2,0:T(4,128)S(1)} %get-tuple-element.8, pred[32,512]{1,0:T(8,128)(4,1)S(1)} %broadcast_compare_fusion), kind=kOutput, calls=%fused_computation.15 | convolution fusion | flops 343932928 | bytes 12353536 | tf_op jit(solution)/shard_map/pksjgl,plkh->pksjgh/dot_general | solution.py:66
  78.1 10.1 %all-to-all-start.2 = ((f32[32,1,16,2,4,80]{5,2,4,3,1,0:T(8,128)}), f32[32,1,16,2,4,80]{5,2,4,3,1,0:T(8,128)}, u32[]{:S(2)}, u32[]{:S(2)}) async-start(f32[32,1,16,2,4,80]{5,2,4,3,1,0:T(8,128)} %fusion.11), calls=%async_computation.2 | async-start | bytes 4194304 | tf_op jit(solution)/shard_map/all_to_all | solution.py:73
  92.9 45.6 %all-to-all-done.2 = f32[32,1,16,2,4,80]{5,2,4,3,1,0:T(8,128)} async-done(((f32[32,1,16,2,4,80]{5,2,4,3,1,0:T(8,128)}), f32[32,1,16,2,4,80]{5,2,4,3,1,0:T(8,128)}, u32[]{:S(2)}, u32[]{:S(2)}) %all-to-all-start.2) | async-done | bytes 1310752 | tf_op jit(solution)/shard_map/all_to_all | solution.py:73
  138.4 1.9 bitcast_reduce_fusion
  140.8 2.5 convolution_convert_fusion.1
  143.4 74.4 %all-reduce.3.cloned.1.call-done = bf16[32,2560]{1,0:T(8,128)(2,1)} async-done(((bf16[32,2560]{1,0:T(8,128)(2,1)}), bf16[32,2560]{1,0:T(8,128)(2,1)}) %all-reduce.3.cloned.1.call-update) | async-done | bytes 163856 | tf_op jit(solution)/shard_map/psum | solution.py:127
  217.8 1.1 multiply_reduce_fusion.2
  219.0 2.4 fusion.45
  221.4 4.3 %convolution_convert_fusion = bf16[32,2560]{1,0:T(8,128)(2,1)} fusion(bf16[512,2560]{1,0:T(8,128)(2,1)} %param.30, bf16[2560,512]{1,0:T(8,128)(2,1)} %param.29, f32[32,512]{1,0:T(8,128)S(1)} %fusion.45, bf16[32,2560]{1,0:T(8,128)(2,1)S(1)} %copy-done.3, bf16[32,2560]{1,0:T(8,128)(2,1)S(1)} %copy-done.2, f32[2560]{0:T(1024)S(1)} %copy-done.6, ...), kind=kOutput, calls=%fused_computation.9 | convolution fusion | flops 168443904 | bytes 5810304 | tf_op jit(solution)/shard_map/dot_general | solution.py:137
  225.8 77.3 %all-reduce.5.cloned.1.call-done = bf16[32,2560]{1,0:T(8,128)(2,1)} async-done(((bf16[32,2560]{1,0:T(8,128)(2,1)}), bf16[32,2560]{1,0:T(8,128)(2,1)}) %all-reduce.5.cloned.1.call-update) | async-done | bytes 163856 | tf_op jit(solution)/shard_map/psum | solution.py:136
  303.1 1.1 multiply_reduce_fusion.1
  304.9 0.7 multiply_reduce_fusion
  (64 shorter events, 6.6 us)
Async XLA Ops:
  7.2 38.4 %copy-start = (bf16[32,512,80]{1,2,0:T(8,128)(2,1)S(1)}, bf16[32,512,80]{1,2,0:T(8,128)(2,1)}, u32[]{:S(2)}) copy-start(bf16[32,512,80]{1,2,0:T(8,128)(2,1)} %param.21) | copy-start | bytes 7864324
  9.0 34.9 %all-to-all-start = ((bf16[32,32,320]{2,1,0:T(8,128)(2,1)}), bf16[32,32,320]{2,1,0:T(8,128)(2,1)S(1)}, u32[]{:S(2)}, u32[]{:S(2)}) async-start(bf16[32,32,320]{2,1,0:T(8,128)(2,1)} %stack.2), calls=%async_computation | async-start | bytes 1572864 | tf_op jit(solution)/shard_map/all_to_all | solution.py:47
  48.4 3.2 %copy-start.1 = (f32[32,16,2,4,512]{4,1,3,2,0:T(8,128)}, f32[32,16,2,4,512]{4,1,3,2,0:T(8,128)S(1)}, u32[]{:S(2)}) copy-start(f32[32,16,2,4,512]{4,1,3,2,0:T(8,128)S(1)} %get-tuple-element.9) | copy-start | bytes 25165828
  52.3 12.1 %all-to-all-start.3 = ((f32[32,1,128]{2,1,0:T(1,128)}), f32[32,1,128]{2,1,0:T(1,128)S(1)}, u32[]{:S(2)}, u32[]{:S(2)}) async-start(f32[32,1,128]{2,1,0:T(1,128)} %reshape.269), calls=%async_computation.3 | async-start | bytes 32768 | tf_op jit(solution)/shard_map/all_to_all | solution.py:75
  64.5 13.6 %all-to-all-start.1 = ((f32[32,1,128]{2,1,0:T(1,128)}), f32[32,1,128]{2,1,0:T(1,128)S(1)}, u32[]{:S(2)}, u32[]{:S(2)}) async-start(f32[32,1,128]{2,1,0:T(1,128)} %reshape.267), calls=%async_computation.1 | async-start | bytes 32768 | tf_op jit(solution)/shard_map/all_to_all | solution.py:74
  78.0 10.2 %copy-start.5 = (bf16[32,320]{1,0:T(8,128)(2,1)S(1)}, bf16[32,320]{1,0:T(8,128)(2,1)}, u32[]{:S(2)}) copy-start(bf16[32,320]{1,0:T(8,128)(2,1)} %param.18) | copy-start | bytes 61444
  78.0 10.3 %copy-start.11 = (bf16[32,80]{1,0:T(8,128)(2,1)S(1)}, bf16[32,80]{1,0:T(8,128)(2,1)}, u32[]{:S(2)}) copy-start(bf16[32,80]{1,0:T(8,128)(2,1)} %param.19) | copy-start | bytes 15364
  78.0 10.8 %copy-start.9 = (s32[1,16]{1,0:T(1,128)S(1)}, s32[1,16]{1,0:T(1,128)}, u32[]{:S(2)}) copy-start(s32[1,16]{1,0:T(1,128)} %param.26) | copy-start | bytes 196
  78.0 10.9 %copy-start.4 = (bf16[1,16,128,80]{2,3,1,0:T(8,128)(2,1)S(1)}, bf16[1,16,128,80]{2,3,1,0:T(8,128)(2,1)}, u32[]{:S(2)}) copy-start(bf16[1,16,128,80]{2,3,1,0:T(8,128)(2,1)} %param.23) | copy-start | bytes 983044
  78.0 14.5 %copy-start.10 = (bf16[1,16,128,80]{2,3,1,0:T(8,128)(2,1)S(1)}, bf16[1,16,128,80]{2,3,1,0:T(8,128)(2,1)}, u32[]{:S(2)}) copy-start(bf16[1,16,128,80]{2,3,1,0:T(8,128)(2,1)} %param.24) | copy-start | bytes 983044
  78.1 60.4 %all-to-all-start.2 = ((f32[32,1,16,2,4,80]{5,2,4,3,1,0:T(8,128)}), f32[32,1,16,2,4,80]{5,2,4,3,1,0:T(8,128)}, u32[]{:S(2)}, u32[]{:S(2)}) async-start(f32[32,1,16,2,4,80]{5,2,4,3,1,0:T(8,128)} %fusion.11), calls=%async_computation.2 | async-start | bytes 4194304 | tf_op jit(solution)/shard_map/all_to_all | solution.py:73
  88.1 129.6 %all-reduce.3.cloned.1.call-start = ((), (), s32[]{:S(2)}) async-start(), calls=%async_computation.4 | async-start | bytes 327680 | tf_op jit(solution)/shard_map/psum | solution.py:127
  88.7 51.7 %copy-start.12 = (bf16[32,80]{1,0:T(8,128)(2,1)S(1)}, bf16[32,80]{1,0:T(8,128)(2,1)}, u32[]{:S(2)}) copy-start(bf16[32,80]{1,0:T(8,128)(2,1)} %param.20) | copy-start | bytes 15364
  140.4 77.4 %copy-start.2 = (bf16[32,2560]{1,0:T(8,128)(2,1)S(1)}, bf16[32,2560]{1,0:T(8,128)(2,1)}, u32[]{:S(2)}) copy-start(bf16[32,2560]{1,0:T(8,128)(2,1)} %param.17) | copy-start | bytes 491524
  140.4 78.6 %copy-start.6 = (f32[2560]{0:T(1024)S(1)}, f32[2560]{0:T(1024)}, u32[]{:S(2)}) copy-start(f32[2560]{0:T(1024)} %param.31) | copy-start | bytes 30724
  143.3 159.7 %all-reduce.5.cloned.1.call-start = ((), (), s32[]{:S(2)}) async-start(), calls=%async_computation.5 | async-start | bytes 327680 | tf_op jit(solution)/shard_map/psum | solution.py:136
  217.8 3.6 %copy-start.3 = (bf16[32,2560]{1,0:T(8,128)(2,1)S(1)}, bf16[32,2560]{1,0:T(8,128)(2,1)}, u32[]{:S(2)}) copy-start(bf16[32,2560]{1,0:T(8,128)(2,1)} %all-reduce.3.cloned.1.call-done) | copy-start | bytes 491524
  221.4 83.5 %copy-start.7 = (f32[2560]{0:T(1024)S(1)}, f32[2560]{0:T(1024)}, u32[]{:S(2)}) copy-start(f32[2560]{0:T(1024)} %param.33) | copy-start | bytes 30724
  221.4 83.4 %copy-start.8 = (f32[2560]{0:T(1024)S(1)}, f32[2560]{0:T(1024)}, u32[]{:S(2)}) copy-start(f32[2560]{0:T(1024)} %param.32) | copy-start | bytes 30724
Sparse Core Ops, SparseCore 0:
  143.4 74.3 all-reduce.2
  225.9 77.1 all-reduce.4
